TPU v7x, 256 devices: a whole 4x4x8 slice. The times are simulated.
256 devices in a mesh: energy: 64 (over z, y, core), atoms: 4 (over x).
Axes of the slice: x: 4, y: 4, z: 8, core: 2. Of those that a mesh axis runs over, the one named last changes fastest.
Arguments:
- green: bfloat16 [1024, 256, 288], P('energy', 'atoms'), may hold values from -6 to 6
- superop: bfloat16 [4, 288, 288], replicated, may hold values from -0.1875 to 0.1875
- phonon: bfloat16 [64, 2048], replicated, may hold values from -0.1875 to 0.1875
- owner: int32 [256, 1], P('atoms'), may hold values from 0 to 63; in each aligned block of 64 rows (0 to 63, 64 to 127, ...) at most 4 rows name the same one
- neighbours: int32 [256, 4], P('atoms'), may hold values from -1 to 255, as said below
Outputs:
- self_energy: bfloat16 [1024, 256, 288], P('energy', 'atoms')
Inputs may be any that keep to these rules, and one draw needn't show every extreme that they name: `owner`: within each aligned block of 64 atoms (one atom group) no domain holds more than 4 atoms, and some domain holds exactly 4. `neighbours`: each entry is -1 or the index of an atom at most 8 away from the row's atom; some entry lies exactly 8 above its row's atom, in the next atom group.
All inputs are finite; a program needn't handle non-finite values.
Results may differ from a plain program's by a relative error of at most 0.0049.
Values may be sent and summed in bfloat16 or wider, within the bound.
No kernel may reach another device: no remote copies, remote signals or barrier semaphores. Data moves between devices by JAX's collectives and lax.ppermute only.
A program may use at most 64 MiB of HBM per device.

v0:
```python
import jax
import jax.numpy as jnp
from jax import lax
from jax.sharding import PartitionSpec as P

SPLIT = 2
HALO = 8
ATOMS_DEV = 1


def padded(block, sides, width):
    for axis, dim in sides:
        count = lax.axis_size(axis)
        forward = [(i, i + 1) for i in range(count - 1)]
        backward = [(target, source) for source, target in forward]
        low = lax.ppermute(
            lax.slice_in_dim(block, block.shape[dim] - width, None, axis=dim), axis, forward
        )
        high = lax.ppermute(lax.slice_in_dim(block, 0, width, axis=dim), axis, backward)
        block = jnp.concatenate([low, block, high], axis=dim)
    return block


def toeplitz_rows(kernel_row, count):
    length = 2 * count
    flipped = kernel_row[::-1]
    tiled = jnp.tile(flipped, count)[: count * (length - 1)]
    return tiled.reshape(count, length - 1)[:, count - 1 : 2 * count - 1]


def per_device(green, superop, phonon, owner, neighbours):
    local_energies = green.shape[0]
    group_size = green.shape[1]
    comps = green.shape[2]
    slots = neighbours.shape[1]
    half_width = comps // SPLIT
    group = lax.axis_index("atoms")
    widened = padded(green, (("atoms", 1),), HALO)
    present = neighbours >= 0
    target_rows = jnp.where(present, neighbours - group * group_size + HALO, 0)
    picked = jnp.take(widened, target_rows.reshape(-1), axis=1)
    picked = jnp.where(present.reshape(1, -1, 1), picked, jnp.zeros_like(picked))
    coupled = jnp.dot(
        picked.reshape(local_energies * group_size, slots * comps),
        superop.reshape(slots * comps, comps),
        preferred_element_type=jnp.float32,
    )
    coupled = coupled.reshape(local_energies, group_size, comps).astype(jnp.bfloat16)
    count = local_energies * lax.axis_size("energy")
    energy_rank = lax.axis_index("energy")
    first_atom = energy_rank * ATOMS_DEV
    mine = lax.dynamic_slice_in_dim(owner[:, 0], first_atom, ATOMS_DEV)

    def build_kernel(domain):
        return toeplitz_rows(phonon[domain], count)

    kernels = jax.vmap(build_kernel)(mine)
    split_blocks = coupled.reshape(local_energies, group_size, SPLIT, half_width)
    product = jnp.einsum(
        "oph,hoiw->poiw",
        kernels,
        lax.all_to_all(split_blocks, "energy", split_axis=1, concat_axis=0, tiled=True),
        preferred_element_type=jnp.float32,
    )
    result = lax.all_to_all(
        product.astype(jnp.bfloat16), "energy", split_axis=0, concat_axis=1, tiled=True
    )
    result = result.reshape(local_energies, group_size, comps)
    return result


def solution(mesh):
    return jax.shard_map(
        per_device,
        mesh=mesh,
        in_specs=(P("energy", "atoms", None), P(), P(), P("atoms", None), P("atoms", None)),
        out_specs=P("energy", "atoms", None),
        check_vma=False,
    )
```

profile of v0, /device:TPU:6, one launch (start us, length us, event | category | flops | bytes accessed | tf_op | source)
XLA Modules:
  0.0 215.0 jit_solution(9396868010489294610)
XLA Ops:
  0.0 0.0 copy-start
  0.0 1.7 copy.36
  1.7 1.3 collective-permute-start
  3.0 4.6 %collective-permute-start.1 = (bf16[16,8,288]{2,0,1:T(8,128)(2,1)S(1)}, bf16[16,8,288]{2,0,1:T(8,128)(2,1)S(1)}, u32[]{:S(2)}, u32[]{:S(2)}) collective-permute-start(bf16[16,8,288]{2,0,1:T(8,128)(2,1)S(1)} %get-tuple-element.19), channel_id=1, source_target_pairs={{1,0},{2,1},{3,2},{5,4},{6,5},{7,6},{9,8},{10,9},{11,10},{13,12},{... | collective-permute-start | bytes 221192 | tf_op jit(solution)/shard_map/ppermute | solution.py:19
  7.6 1.2 constant_dynamic-slice_fusion.1
  10.8 0.8 constant_dynamic-slice_fusion
  11.5 1.5 reverse
  13.0 0.5 broadcast_bitcast_fusion
  13.5 0.0 copy-start.1
  13.6 24.7 %copy.51 = bf16[1,1,1024,2048]{3,1,2,0:T(2,128)(2,1)} copy(bf16[1,1,1024,2048]{3,2,1,0:T(8,128)(2,1)S(1)} %broadcast_bitcast_fusion) | data formatting | bytes 8388608
  38.2 0.0 copy-done.1
  38.2 0.1 copy.39
  38.3 0.1 reshape.125
  38.5 0.1 copy.34
  38.6 0.1 broadcast_in_dim.34
  38.7 0.1 broadcast_in_dim.35
  38.8 0.1 copy.35
  38.9 0.1 broadcast_in_dim.37
  39.1 0.1 broadcast_in_dim.38
  39.2 0.0 collective-permute-done
  39.2 0.0 collective-permute-done.1
  39.2 0.2 pad_maximum_fusion
  39.4 2.8 %gather_fusion = bf16[256,16,288]{2,1,0:T(8,128)(2,1)} fusion(bf16[16,80,288]{2,0,1:T(8,128)(2,1)S(1)} %pad_maximum_fusion, s32[1024]{0:T(1024)S(1)} %pad_clamp_fusion), kind=kCustom, calls=%fused_computation | custom fusion | bytes 4719616 | tf_op jit(solution)/shard_map/jit(_take)/gather | solution.py:41
  42.2 3.2 %select_bitcast_fusion = bf16[16,256,288]{2,0,1:T(8,128)(2,1)S(1)} fusion(bf16[256,16,288]{2,1,0:T(8,128)(2,1)} %gather_fusion, pred[256,288]{1,0:T(8,128)(4,1)S(1)} %broadcast_in_dim.35, pred[256,288]{1,0:T(8,128)(4,1)S(1)} %broadcast_in_dim.38), kind=kLoop, calls=%fused_computation.2 | loop fusion | flops 2359296 | bytes 4866048 | tf_op jit(solution)/shard_map/jit(_where)/select_n | solution.py:42
  45.4 2.5 %copy.40 = bf16[16,256,288]{2,1,0:T(8,128)(2,1)} copy(bf16[16,256,288]{2,0,1:T(8,128)(2,1)S(1)} %select_bitcast_fusion) | data formatting | bytes 4718592 | tf_op jit(solution)/shard_map/jit(_where)/select_n | solution.py:42
  47.9 5.8 %select_n.60 = bf16[16,64,1152]{2,1,0:T(8,128)(2,1)S(1)} reshape(bf16[16,256,288]{2,1,0:T(8,128)(2,1)} %copy.40) | data formatting | bytes 4718592 | tf_op jit(solution)/shard_map/jit(_where)/select_n | solution.py:42
  53.7 0.0 copy-done
  53.7 2.3 %convolution_convert_fusion = bf16[16,64,288]{2,1,0:T(8,128)(2,1)} fusion(bf16[16,64,1152]{2,1,0:T(8,128)(2,1)S(1)} %select_n.60, bf16[1152,288,1]{1,0,2:T(8,128)(2,1)S(1)} %bitcast.36), kind=kOutput, calls=%fused_computation.6 | convolution fusion | flops 679772160 | bytes 3612672 | tf_op jit(solution)/shard_map/dot_general | solution.py:43
  56.0 3.1 %reshape.127 = bf16[16,64,2,144]{3,2,1,0:T(2,128)(2,1)S(1)} reshape(bf16[16,64,288]{2,1,0:T(8,128)(2,1)} %convolution_convert_fusion) | data formatting | bytes 1179648 | tf_op jit(solution)/shard_map/reshape | solution.py:58
  59.2 2.2 %copy.42 = bf16[16,64,2,144]{3,0,2,1:T(8,128)(2,1)} copy(bf16[16,64,2,144]{3,2,1,0:T(2,128)(2,1)S(1)} %reshape.127) | data formatting | bytes 1179648 | tf_op jit(solution)/shard_map/reshape | solution.py:58
  61.4 12.3 %all-to-all-start = ((bf16[16,64,2,144]{3,0,2,1:T(8,128)(2,1)}), bf16[16,64,2,144]{3,0,2,1:T(8,128)(2,1)S(1)}, u32[]{:S(2)}, u32[]{:S(2)}) async-start(bf16[16,64,2,144]{3,0,2,1:T(8,128)(2,1)} %copy.42), calls=%async_computation | async-start | bytes 2097152 | tf_op jit(solution)/shard_map/all_to_all | solution.py:62
  73.7 84.7 %slice_reduce_fusion = bf16[2096128]{0:T(1024)(128)(2,1)} fusion(bf16[1,2097152]{1,0:T(2,128)(2,1)} %bitcast.37), kind=kLoop, calls=%fused_computation.1 | loop fusion | bytes 8384512 | tf_op jit(solution)/shard_map/vmap()/slice | solution.py:27
  158.4 10.7 %reshape.129 = bf16[1,1024,2047]{2,1,0:T(8,128)(2,1)} reshape(bf16[2096128]{0:T(1024)(128)(2,1)} %slice_reduce_fusion) | data formatting | bytes 8384512 | tf_op jit(solution)/shard_map/vmap()/reshape | solution.py:28
  169.0 0.0 all-to-all-done
  169.0 0.1 copy.43
  169.1 3.6 %fusion.2 = bf16[1024,1,2,144]{0,3,2,1:T(8,128)(2,1)S(1)} fusion(bf16[1024,2,144]{2,0,1:T(8,128)(2,1)S(1)} %bitcast.40, bf16[1,1024,2047]{2,1,0:T(8,128)(2,1)} %reshape.129), kind=kOutput, calls=%fused_computation.8 | convolution fusion | flops 604274688 | bytes 3276800 | tf_op jit(solution)/shard_map/oph,hoiw->poiw/dot_general | solution.py:59
  172.7 0.9 copy.45
  173.6 38.8 %all_to_all.30 = bf16[1024,1,2,144]{3,2,1,0:T(2,128)(2,1)S(1)} all-to-all(bf16[1024,1,2,144]{3,2,1,0:T(2,128)(2,1)S(1)} %copy.45), channel_id=1, replica_groups=mesh['energy'=64,'atoms'=4] {'energy'}, dimensions={0} | all-to-all | bytes 1179648 | tf_op jit(solution)/shard_map/all_to_all | solution.py:65
  212.4 0.1 copy.46
  212.5 1.1 copy.47
  213.6 1.4 reshape.131
  (5 shorter events, 0.1 us)
Async XLA Ops:
  0.0 53.7 %copy-start = (bf16[4,288,288]{2,1,0:T(8,128)(2,1)S(1)}, bf16[4,288,288]{2,1,0:T(8,128)(2,1)}, u32[]{:S(2)}) copy-start(bf16[4,288,288]{2,1,0:T(8,128)(2,1)} %param.6) | copy-start | bytes 1990660
  1.7 37.5 %collective-permute-start = (bf16[16,8,288]{2,0,1:T(8,128)(2,1)S(1)}, bf16[16,8,288]{2,0,1:T(8,128)(2,1)S(1)}, u32[]{:S(2)}, u32[]{:S(2)}) collective-permute-start(bf16[16,8,288]{2,0,1:T(8,128)(2,1)S(1)} %get-tuple-element.18), channel_id=1, source_target_pairs={{0,1},{1,2},{2,3},{4,5},{5,6},{6,7},{8,9},{9,10},{10,11},{12,13},{... | collective-permute-start | bytes 221192 | tf_op jit(solution)/shard_map/ppermute | solution.py:16
  3.0 36.2 %collective-permute-start.1 = (bf16[16,8,288]{2,0,1:T(8,128)(2,1)S(1)}, bf16[16,8,288]{2,0,1:T(8,128)(2,1)S(1)}, u32[]{:S(2)}, u32[]{:S(2)}) collective-permute-start(bf16[16,8,288]{2,0,1:T(8,128)(2,1)S(1)} %get-tuple-element.19), channel_id=1, source_target_pairs={{1,0},{2,1},{3,2},{5,4},{6,5},{7,6},{9,8},{10,9},{11,10},{13,12},{... | collective-permute-start | bytes 221192 | tf_op jit(solution)/shard_map/ppermute | solution.py:19
  13.5 24.7 %copy-start.1 = (s32[64,4]{0,1:T(4,128)S(1)}, s32[64,4]{0,1:T(4,128)}, u32[]{:S(2)}) copy-start(s32[64,4]{0,1:T(4,128)} %param.9) | copy-start | bytes 3076
  61.4 107.6 %all-to-all-start = ((bf16[16,64,2,144]{3,0,2,1:T(8,128)(2,1)}), bf16[16,64,2,144]{3,0,2,1:T(8,128)(2,1)S(1)}, u32[]{:S(2)}, u32[]{:S(2)}) async-start(bf16[16,64,2,144]{3,0,2,1:T(8,128)(2,1)} %copy.42), calls=%async_computation | async-start | bytes 2097152 | tf_op jit(solution)/shard_map/all_to_all | solution.py:62
where the time goes:
time: 216 us; the launch traced here: 215 us
  local copies, waits for them, and re-layouts  147 us (68%)
  blocking collectives  38.8 us (18%)
  starting transfers between devices  18.1 us (8%)
  matrix products  5.92 us (3%)
  other arithmetic  3.44 us (2%)
    slice x1, local copies, waits for them, and re-layouts, toeplitz_rows(): tiled = jnp.tile(flipped, count)[:count * (length - 1)]  84.7 us
    all_to_all x1, blocking collectives, per_device(): lax.all_to_all(product.astype(jnp.bfloat16), 'energy', split_axis=0, conc...  38.8 us
    unnamed x8, local copies, waits for them, and re-layouts  28.3 us
    all_to_all x1, starting transfers between devices, per_device(): lax.all_to_all(split_blocks, 'energy', split_axis=1, concat_axis=0, tiled...  12.3 us
    reshape x1, local copies, waits for them, and re-layouts, toeplitz_rows(): return tiled.reshape(count, length - 1)[:, count - 1:2 * count - 1]  10.7 us
    select_n x2, local copies, waits for them, and re-layouts, per_device(): jnp.where(present.reshape(1, -1, 1), picked, jnp.zeros_like(picked))  8.28 us
    reshape x2, local copies, waits for them, and re-layouts, per_device(): coupled.reshape(local_energies, group_size, SPLIT, half_width)  5.32 us
    ppermute x1, starting transfers between devices, padded(): lax.ppermute(lax.slice_in_dim(block, 0, width, axis=dim), axis, backward)  4.55 us
  transfers between devices with their start and end apart: 3, of which 0 were waited for; matrix products, arithmetic and copies ran while one was open for 58% of the time, Pallas kernels for 0%

commit v1 on v0

--- a/solution.py
+++ b/solution.py
@@ -1,3 +1,4 @@
+import functools
 import jax
 import jax.numpy as jnp
 from jax import lax
@@ -6,6 +7,17 @@
 SPLIT = 2
 HALO = 8
 ATOMS_DEV = 1
+
+
+def _resolve_halves(load, in_dim, dimension_no):
+    outcome_arr = jax.lax.axis_size("energy")
+    block_now = jnp.split(load, outcome_arr, axis=in_dim)
+    n_now = jnp.stack(block_now, axis=0)
+    out_arr = jax.lax.all_to_all(n_now, "energy", 0, 0)
+    return jnp.concatenate(out_arr, axis=dimension_no)
+
+
+report_sheet_now = functools.partial(_resolve_halves, in_dim=0, dimension_no=1)
 
 
 def padded(block, sides, width):
@@ -62,9 +74,7 @@
         lax.all_to_all(split_blocks, "energy", split_axis=1, concat_axis=0, tiled=True),
         preferred_element_type=jnp.float32,
     )
-    result = lax.all_to_all(
-        product.astype(jnp.bfloat16), "energy", split_axis=0, concat_axis=1, tiled=True
-    )
+    result = report_sheet_now(product.astype(jnp.bfloat16))
     result = result.reshape(local_energies, group_size, comps)
     return result
 

time: 216 us -> 319 us (1.48); the launches traced: 215 us -> 314 us
  local copies, waits for them, and re-layouts: 147 us -> 245 us
    another operation x0 -> x70, local copies, waits for them, and re-layouts: none -> 72.5 us  [the longest x69 71.1 us: _resolve_halves(): n_now = jnp.stack(block_now, axis=0)]
    unnamed x8 -> x77, local copies, waits for them, and re-layouts: 28.3 us -> 57.2 us
  transfers between devices with their start and end apart: 3 -> 3, of which waited for: 0 -> 0; matrix products, arithmetic and copies ran while one was open for 58% -> 40% of each run, Pallas kernels for 0% -> 0%
where the time goes in v1:
time: 319 us; the launch traced here: 314 us
  local copies, waits for them, and re-layouts  245 us (77%)
  blocking collectives  38.8 us (12%)
  starting transfers between devices  18.1 us (6%)
  matrix products  5.92 us (2%)
  other arithmetic  3.44 us (1%)
    slice x1, local copies, waits for them, and re-layouts, toeplitz_rows(): tiled = jnp.tile(flipped, count)[:count * (length - 1)]  84.7 us
    another operation x69, local copies, waits for them, and re-layouts, _resolve_halves(): n_now = jnp.stack(block_now, axis=0)  71.1 us
    unnamed x77, local copies, waits for them, and re-layouts  57.2 us
    all_to_all x1, blocking collectives, _resolve_halves(): out_arr = jax.lax.all_to_all(n_now, 'energy', 0, 0)  38.8 us
    all_to_all x1, starting transfers between devices, per_device(): lax.all_to_all(split_blocks, 'energy', split_axis=1, concat_axis=0, tiled...  12.3 us
    reshape x1, local copies, waits for them, and re-layouts, toeplitz_rows(): return tiled.reshape(count, length - 1)[:, count - 1:2 * count - 1]  10.7 us
    select_n x2, local copies, waits for them, and re-layouts, per_device(): jnp.where(present.reshape(1, -1, 1), picked, jnp.zeros_like(picked))  8.25 us
  transfers between devices with their start and end apart: 3, of which 0 were waited for; matrix products, arithmetic and copies ran while one was open for 40% of the time, Pallas kernels for 0%

profile of v1, /device:TPU:6, one launch (start us, length us, event | category | flops | bytes accessed | tf_op | source)
XLA Modules:
  0.0 314.1 jit_solution(2096782755567653543)
XLA Ops:
  0.0 1.7 copy.99
  3.0 4.6 %collective-permute-start.1 = (bf16[16,8,288]{2,0,1:T(8,128)(2,1)S(1)}, bf16[16,8,288]{2,0,1:T(8,128)(2,1)S(1)}, u32[]{:S(2)}, u32[]{:S(2)}) collective-permute-start(bf16[16,8,288]{2,0,1:T(8,128)(2,1)S(1)} %get-tuple-element.19), channel_id=1, source_target_pairs={{1,0},{2,1},{3,2},{5,4},{6,5},{7,6},{9,8},{10,9},{11,10},{13,12},{... | collective-permute-start | bytes 221192 | tf_op jit(solution)/shard_map/ppermute | solution.py:31
  13.6 24.7 %copy.176 = bf16[1,1,1024,2048]{3,1,2,0:T(2,128)(2,1)} copy(bf16[1,1,1024,2048]{3,2,1,0:T(8,128)(2,1)S(1)} %broadcast_bitcast_fusion) | data formatting | bytes 8388608
  39.4 2.8 gather_fusion
  42.2 3.2 %select_bitcast_fusion = bf16[16,256,288]{2,0,1:T(8,128)(2,1)S(1)} fusion(bf16[256,16,288]{2,1,0:T(8,128)(2,1)} %gather_fusion, pred[256,288]{1,0:T(8,128)(4,1)S(1)} %broadcast_in_dim.35, pred[256,288]{1,0:T(8,128)(4,1)S(1)} %broadcast_in_dim.38), kind=kLoop, calls=%fused_computation.2 | loop fusion | flops 2359296 | bytes 4866048 | tf_op jit(solution)/shard_map/jit(_where)/select_n | solution.py:54
  45.4 2.4 copy.103
  47.9 5.8 %select_n.60 = bf16[16,64,1152]{2,1,0:T(8,128)(2,1)S(1)} reshape(bf16[16,256,288]{2,1,0:T(8,128)(2,1)} %copy.103) | data formatting | bytes 4718592 | tf_op jit(solution)/shard_map/jit(_where)/select_n | solution.py:54
  53.7 2.3 convolution_convert_fusion
  56.0 3.1 %reshape.126 = bf16[16,64,2,144]{3,2,1,0:T(2,128)(2,1)S(1)} reshape(bf16[16,64,288]{2,1,0:T(8,128)(2,1)} %convolution_convert_fusion) | data formatting | bytes 1179648 | tf_op jit(solution)/shard_map/reshape | solution.py:70
  59.1 2.2 copy.105
  61.3 12.3 %all-to-all-start = ((bf16[16,64,2,144]{3,0,2,1:T(8,128)(2,1)}), bf16[16,64,2,144]{3,0,2,1:T(8,128)(2,1)S(1)}, u32[]{:S(2)}, u32[]{:S(2)}) async-start(bf16[16,64,2,144]{3,0,2,1:T(8,128)(2,1)} %copy.105), calls=%async_computation | async-start | bytes 2097152 | tf_op jit(solution)/shard_map/all_to_all | solution.py:74
  73.6 84.7 %slice_reduce_fusion = bf16[2096128]{0:T(1024)(128)(2,1)} fusion(bf16[1,2097152]{1,0:T(2,128)(2,1)} %bitcast.163), kind=kLoop, calls=%fused_computation.1 | loop fusion | bytes 8384512 | tf_op jit(solution)/shard_map/vmap()/slice | solution.py:39
  158.3 10.7 %reshape.128 = bf16[1,1024,2047]{2,1,0:T(8,128)(2,1)} reshape(bf16[2096128]{0:T(1024)(128)(2,1)} %slice_reduce_fusion) | data formatting | bytes 8384512 | tf_op jit(solution)/shard_map/vmap()/reshape | solution.py:40
  169.1 3.6 %fusion.2 = bf16[1024,1,2,144]{0,3,2,1:T(8,128)(2,1)S(1)} fusion(bf16[1024,2,144]{2,0,1:T(8,128)(2,1)S(1)} %bitcast.166, bf16[1,1024,2047]{2,1,0:T(8,128)(2,1)} %reshape.128), kind=kOutput, calls=%fused_computation.8 | convolution fusion | flops 604274688 | bytes 3276800 | tf_op jit(solution)/shard_map/oph,hoiw->poiw/dot_general | solution.py:71
  178.2 1.6 copy.109
  179.8 1.6 copy.110
  181.3 1.6 copy.111
  182.9 1.6 copy.112
  184.5 1.6 copy.113
  187.6 1.6 copy.115
  189.1 1.6 copy.116
  190.7 1.6 copy.117
  192.2 1.6 copy.118
  193.8 1.6 copy.119
  195.4 1.6 copy.120
  196.9 1.6 copy.121
  198.5 1.6 copy.122
  203.1 1.6 copy.125
  206.3 1.6 copy.127
  209.4 1.6 copy.129
  210.9 1.6 copy.130
  212.5 1.6 copy.131
  214.0 1.6 copy.132
  215.6 1.6 copy.133
  217.2 1.6 copy.134
  218.7 1.6 copy.135
  220.3 1.6 copy.136
  221.8 1.6 copy.137
  223.4 1.6 copy.138
  224.9 1.6 copy.139
  228.1 1.6 copy.141
  229.6 1.6 copy.142
  231.2 1.6 copy.143
  235.8 1.6 copy.146
  237.4 1.6 copy.147
  239.0 1.6 copy.148
  240.5 1.6 copy.149
  272.9 38.8 %all_to_all.20 = bf16[64,16,1,2,144]{4,1,3,2,0:T(8,128)(2,1)S(1)} all-to-all(bf16[64,16,1,2,144]{4,1,3,2,0:T(8,128)(2,1)S(1)} %constant_dynamic-update-slice_fusion), channel_id=1, replica_groups=mesh['energy'=64,'atoms'=4] {'energy'}, dimensions={0} | all-to-all | bytes 1179648 | tf_op jit(solution)/shard_map/all_to_all | solution.py:16
  (134 shorter events, 57.5 us)
Async XLA Ops:
  0.0 53.7 %copy-start = (bf16[4,288,288]{2,1,0:T(8,128)(2,1)S(1)}, bf16[4,288,288]{2,1,0:T(8,128)(2,1)}, u32[]{:S(2)}) copy-start(bf16[4,288,288]{2,1,0:T(8,128)(2,1)} %param.6) | copy-start | bytes 1990660
  1.7 37.5 %collective-permute-start = (bf16[16,8,288]{2,0,1:T(8,128)(2,1)S(1)}, bf16[16,8,288]{2,0,1:T(8,128)(2,1)S(1)}, u32[]{:S(2)}, u32[]{:S(2)}) collective-permute-start(bf16[16,8,288]{2,0,1:T(8,128)(2,1)S(1)} %get-tuple-element.18), channel_id=1, source_target_pairs={{0,1},{1,2},{2,3},{4,5},{5,6},{6,7},{8,9},{9,10},{10,11},{12,13},{... | collective-permute-start | bytes 221192 | tf_op jit(solution)/shard_map/ppermute | solution.py:28
  3.0 36.2 %collective-permute-start.1 = (bf16[16,8,288]{2,0,1:T(8,128)(2,1)S(1)}, bf16[16,8,288]{2,0,1:T(8,128)(2,1)S(1)}, u32[]{:S(2)}, u32[]{:S(2)}) collective-permute-start(bf16[16,8,288]{2,0,1:T(8,128)(2,1)S(1)} %get-tuple-element.19), channel_id=1, source_target_pairs={{1,0},{2,1},{3,2},{5,4},{6,5},{7,6},{9,8},{10,9},{11,10},{13,12},{... | collective-permute-start | bytes 221192 | tf_op jit(solution)/shard_map/ppermute | solution.py:31
  13.5 24.7 %copy-start.4 = (s32[64,4]{0,1:T(4,128)S(1)}, s32[64,4]{0,1:T(4,128)}, u32[]{:S(2)}) copy-start(s32[64,4]{0,1:T(4,128)} %param.9) | copy-start | bytes 3076
  61.3 107.7 %all-to-all-start = ((bf16[16,64,2,144]{3,0,2,1:T(8,128)(2,1)}), bf16[16,64,2,144]{3,0,2,1:T(8,128)(2,1)S(1)}, u32[]{:S(2)}, u32[]{:S(2)}) async-start(bf16[16,64,2,144]{3,0,2,1:T(8,128)(2,1)} %copy.105), calls=%async_computation | async-start | bytes 2097152 | tf_op jit(solution)/shard_map/all_to_all | solution.py:74
  242.8 29.8 %copy-start.3 = (bf16[1,16,1,2,144]{4,1,3,2,0:T(8,128)(2,1)S(1)}, bf16[1,16,1,2,144]{4,1,3,2,0:T(8,128)(2,1)}, u32[]{:S(2)}) copy-start(bf16[1,16,1,2,144]{4,1,3,2,0:T(8,128)(2,1)} %copy.148) | copy-start | bytes 27652
  242.8 29.8 %copy-start.2 = (bf16[1,16,1,2,144]{4,1,3,2,0:T(8,128)(2,1)S(1)}, bf16[1,16,1,2,144]{4,1,3,2,0:T(8,128)(2,1)}, u32[]{:S(2)}) copy-start(bf16[1,16,1,2,144]{4,1,3,2,0:T(8,128)(2,1)} %copy.149) | copy-start | bytes 27652
  242.8 29.8 %copy-start.1 = (bf16[1,16,1,2,144]{4,1,3,2,0:T(8,128)(2,1)S(1)}, bf16[1,16,1,2,144]{4,1,3,2,0:T(8,128)(2,1)}, u32[]{:S(2)}) copy-start(bf16[1,16,1,2,144]{4,1,3,2,0:T(8,128)(2,1)} %copy.150) | copy-start | bytes 27652
